TPU v7x, 32 devices: a whole 2x2x4 slice. The times are simulated.
32 devices in a mesh: dp: 8 (over z, x), tensor: 4 (over y, core).
Axes of the slice: x: 2, y: 2, z: 4, core: 2. Of those that a mesh axis runs over, the one named last changes fastest.
Arguments:
- tokens: bfloat16 [2048, 4096], P('dp', 'tensor'), may hold values from -6 to 6
- norm_gain: float32 [4096], replicated, may hold values from 0.15 to 5.4, as said below
- w_query: bfloat16 [4096, 4096], P(None, 'tensor'), may hold values from -0.09375 to 0.09375
- key_weight: bfloat16 [4096, 1024], P(None, 'tensor'), may hold values from -0.09375 to 0.09375
- value_weight: bfloat16 [4096, 1024], P(None, 'tensor'), may hold values from -0.09375 to 0.09375
- w_out: bfloat16 [4096, 4096], P('tensor'), may hold values from -0.25 to 0.25
- grad_output: bfloat16 [2048, 4096], P('dp', 'tensor'), may hold values from -6 to 6
- doc_lengths: int32 [8, 2], P('dp'), may hold values from 0 to 256, as said below
- block_owner: int32 [8, 8], replicated, may hold values from 0 to 7, as said below
Outputs:
- relaid_output: bfloat16 [2048, 4096], P('dp', 'tensor')
- input_grad: bfloat16 [2048, 4096], P('dp', 'tensor')
Inputs may be any that keep to these rules, and one draw needn't show every extreme that they name: `doc_lengths`: each row lists the lengths of the documents packed on that dp index in order: multiples of 128, the nonzero ones first, summing to 256. In every draw some dp index holds a single document of 256 tokens. `block_owner`: every dp index owns exactly one block of each position j < 8 and exactly one block from each dp index. `norm_gain`: positive gains.
All inputs are finite; a program needn't handle non-finite values.
Results may differ from a plain program's by a relative error of at most 0.015.
Values may be sent and summed in bfloat16 or wider, within the bound.
No kernel may reach another device: no remote copies, remote signals or barrier semaphores. Data moves between devices by JAX's collectives and lax.ppermute only.
A program may use at most 128 MiB of HBM per device.

v0:
```python
import math
import jax
import jax.numpy as jnp
from jax import lax
from jax.sharding import PartitionSpec as P

HEAD_SIZE = 128
ROPE_BASE = 500000.0
NORM_EPSILON = 1e-05


def doc_tables(lengths_row, token_row_count):
    ends = jnp.cumsum(lengths_row)
    token_index = jnp.arange(token_row_count, dtype=jnp.int32)
    passed = (token_index[:, None] >= ends[None, :]).astype(jnp.int32)
    doc_ids = jnp.sum(passed, axis=1)
    starts = jnp.max(jnp.where(passed > 0, ends[None, :], 0), axis=1)
    return (doc_ids, token_index - starts)


def rope_tables(positions, head_size):
    half_dim = head_size // 2
    steps = jnp.arange(half_dim, dtype=jnp.float32)
    inverse_freq = jnp.power(ROPE_BASE, -2.0 * steps / head_size)
    angles = positions.astype(jnp.float32)[:, None] * inverse_freq[None, :]
    return (jnp.cos(angles), jnp.sin(angles))


def rotate(vectors, cosine, sine_table):
    half_dim = vectors.shape[-1] // 2
    former = vectors[..., :half_dim]
    latter = vectors[..., half_dim:]
    cos_part = cosine[:, None, :]
    sin_part = sine_table[:, None, :]
    return jnp.concatenate(
        [former * cos_part - latter * sin_part, latter * cos_part + former * sin_part], axis=-1
    )


def unrotate(vectors, cosine, sine_table):
    half_dim = vectors.shape[-1] // 2
    former = vectors[..., :half_dim]
    latter = vectors[..., half_dim:]
    cos_part = cosine[:, None, :]
    sin_part = sine_table[:, None, :]
    return jnp.concatenate(
        [former * cos_part + latter * sin_part, latter * cos_part - former * sin_part], axis=-1
    )


def per_device(
    tokens,
    norm_gain,
    w_query,
    key_weight,
    value_weight,
    w_out,
    grad_output,
    doc_lengths,
    block_owner,
):
    token_row_count, width_part = tokens.shape
    full_width = norm_gain.shape[0]
    sources = lax.axis_size("dp")
    data_index = lax.axis_index("dp")
    tensor_index = lax.axis_index("tensor")
    query_width = w_query.shape[1]
    key_width = key_weight.shape[1]
    heads_local = query_width // HEAD_SIZE
    kv_local = key_width // HEAD_SIZE
    query_group_width = heads_local // kv_local
    scale_factor = 1.0 / math.sqrt(HEAD_SIZE)
    gain_part = lax.dynamic_slice_in_dim(norm_gain, tensor_index * width_part, width_part)
    w_joined = jnp.concatenate([w_query, key_weight, value_weight], axis=1)
    x_float = tokens.astype(jnp.float32)
    gathered = lax.all_gather(tokens, "tensor", axis=1, tiled=True)
    gathered_float = gathered.astype(jnp.float32)
    inverse = lax.rsqrt(jnp.mean(gathered_float * gathered_float, axis=1) + NORM_EPSILON)
    normed_input = (gathered_float * inverse[:, None] * norm_gain[None, :]).astype(jnp.bfloat16)
    projected = jnp.dot(normed_input, w_joined, preferred_element_type=jnp.float32)
    doc_ids, positions = doc_tables(doc_lengths[0], token_row_count)
    token_index = jnp.arange(token_row_count, dtype=jnp.int32)
    allowed = (doc_ids[:, None] == doc_ids[None, :]) & (
        token_index[None, :] <= token_index[:, None]
    )
    cosine, sine_table = rope_tables(positions, HEAD_SIZE)
    query_rows = rotate(
        projected[:, :query_width].reshape(token_row_count, heads_local, HEAD_SIZE),
        cosine,
        sine_table,
    ).astype(jnp.bfloat16)
    keys = rotate(
        projected[:, query_width : query_width + key_width].reshape(
            token_row_count, kv_local, HEAD_SIZE
        ),
        cosine,
        sine_table,
    ).astype(jnp.bfloat16)
    value_rows = (
        projected[:, query_width + key_width :]
        .astype(jnp.bfloat16)
        .reshape(token_row_count, kv_local, HEAD_SIZE)
    )
    grouped_query = query_rows.reshape(token_row_count, kv_local, query_group_width, HEAD_SIZE)
    scores = (
        jnp.einsum("qkgd,skd->kgqs", grouped_query, keys, preferred_element_type=jnp.float32)
        * scale_factor
    )
    weights = jnp.where(allowed[None, None], jnp.exp(scores), 0.0)
    probs = weights / jnp.sum(weights, axis=-1, keepdims=True)
    probs_low = probs.astype(jnp.bfloat16)
    attended = jnp.einsum(
        "kgqs,skd->qkgd", probs_low, value_rows, preferred_element_type=jnp.float32
    ).astype(jnp.bfloat16)
    attended_flat = attended.reshape(token_row_count, query_width)
    mixed_turned = lax.psum_scatter(
        lax.dot_general(
            w_out, attended_flat, (((0,), (1,)), ((), ())), preferred_element_type=jnp.float32
        ).astype(jnp.bfloat16),
        "tensor",
        scatter_dimension=0,
        tiled=True,
    ).astype(jnp.float32)
    output_home = (x_float + mixed_turned.T).astype(jnp.bfloat16)
    block_count = block_owner.shape[1]
    owner_row = lax.dynamic_slice_in_dim(block_owner, data_index, 1, 0)[0]
    slot_index = jnp.arange(sources, dtype=jnp.int32)
    send_table = (owner_row[None, :] == slot_index[:, None]).astype(jnp.bfloat16)
    owned_flags = jnp.sum((block_owner == data_index).astype(jnp.int32), axis=1)
    owned_rank = jnp.cumsum(owned_flags) - owned_flags
    block_index = jnp.arange(block_count, dtype=jnp.int32)
    keep_table = (
        (owned_rank[None, :] == block_index[:, None]) & (owned_flags[None, :] > 0)
    ).astype(jnp.bfloat16)
    home_blocks = output_home.reshape(block_count, -1)
    outgoing = jnp.dot(send_table, home_blocks, preferred_element_type=jnp.float32).astype(
        jnp.bfloat16
    )
    incoming = lax.all_to_all(outgoing, "dp", split_axis=0, concat_axis=0, tiled=True)
    relaid = (
        jnp.dot(keep_table, incoming, preferred_element_type=jnp.float32)
        .astype(jnp.bfloat16)
        .reshape(token_row_count, width_part)
    )
    owned_blocks = grad_output.reshape(block_count, -1)
    returning = lax.dot_general(
        keep_table, owned_blocks, (((0,), (0,)), ((), ())), preferred_element_type=jnp.float32
    ).astype(jnp.bfloat16)
    arrived = lax.all_to_all(returning, "dp", split_axis=0, concat_axis=0, tiled=True)
    grad_home = (
        lax.dot_general(
            send_table, arrived, (((0,), (0,)), ((), ())), preferred_element_type=jnp.float32
        )
        .astype(jnp.bfloat16)
        .reshape(token_row_count, width_part)
    )
    attended_gradient = lax.dot_general(
        lax.all_gather(grad_home, "tensor", axis=1, tiled=True),
        w_out,
        (((1,), (1,)), ((), ())),
        preferred_element_type=jnp.float32,
    ).astype(jnp.bfloat16)
    grouped_gradient = attended_gradient.reshape(
        token_row_count, kv_local, query_group_width, HEAD_SIZE
    )
    delta = jnp.sum(grouped_gradient.astype(jnp.float32) * attended.astype(jnp.float32), axis=-1)
    grad_probs = jnp.einsum(
        "qkgd,skd->kgqs", grouped_gradient, value_rows, preferred_element_type=jnp.float32
    )
    grad_scores = (probs * (grad_probs - jnp.transpose(delta, (1, 2, 0))[..., None])).astype(
        jnp.bfloat16
    )
    grad_query_rot = (
        jnp.einsum("kgqs,skd->qkgd", grad_scores, keys, preferred_element_type=jnp.float32)
        * scale_factor
    )
    grad_keys_rot = (
        jnp.einsum("kgqs,qkgd->skd", grad_scores, grouped_query, preferred_element_type=jnp.float32)
        * scale_factor
    )
    value_gradient = jnp.einsum(
        "kgqs,qkgd->skd", probs_low, grouped_gradient, preferred_element_type=jnp.float32
    )
    grad_query = unrotate(
        grad_query_rot.reshape(token_row_count, heads_local, HEAD_SIZE), cosine, sine_table
    ).astype(jnp.bfloat16)
    key_gradient = unrotate(grad_keys_rot, cosine, sine_table).astype(jnp.bfloat16)
    joined_grad = jnp.concatenate(
        [
            grad_query.reshape(token_row_count, query_width),
            key_gradient.reshape(token_row_count, key_width),
            value_gradient.astype(jnp.bfloat16).reshape(token_row_count, key_width),
        ],
        axis=1,
    )
    normed_gradient = (
        lax.psum_scatter(
            lax.dot_general(
                w_joined, joined_grad, (((1,), (1,)), ((), ())), preferred_element_type=jnp.float32
            ).astype(jnp.bfloat16),
            "tensor",
            scatter_dimension=0,
            tiled=True,
        )
        .astype(jnp.float32)
        .T
    )
    stat = (
        lax.psum(jnp.sum(normed_gradient * gain_part[None, :] * x_float, axis=1), "tensor")
        / full_width
    )
    cubed = inverse * inverse * inverse
    grad_x = (
        grad_home.astype(jnp.float32)
        + inverse[:, None] * gain_part[None, :] * normed_gradient
        - x_float * cubed[:, None] * stat[:, None]
    )
    return (relaid, grad_x.astype(jnp.bfloat16))


def solution(mesh):
    placed = (
        P("dp", "tensor"),
        P(),
        P(None, "tensor"),
        P(None, "tensor"),
        P(None, "tensor"),
        P("tensor", None),
        P("dp", "tensor"),
        P("dp", None),
        P(),
    )
    return jax.shard_map(
        per_device,
        mesh=mesh,
        in_specs=placed,
        out_specs=(P("dp", "tensor"), P("dp", "tensor")),
        check_vma=False,
    )
```

profile of v0, /device:TPU:0, one launch (start us, length us, event | category | flops | bytes accessed | tf_op | source)
XLA Modules:
  0.0 188.4 jit_solution(454758210394766941)
XLA Ops:
  7.2 0.7 all-gather.3.cloned.1.call-update
  7.9 1.3 reshape.232
  9.2 0.8 convert_reduce_fusion
  10.0 0.2 reduce-window.16
  10.2 0.4 fusion.1
  10.6 0.6 broadcast.110
  11.1 1.1 reduce
  12.2 1.2 reshape.245
  13.4 7.3 %all-to-all-start.1 = ((bf16[8,2,16384]{2,1,0:T(2,128)(2,1)}), bf16[8,2,16384]{2,1,0:T(2,128)(2,1)S(1)}, u32[]{:S(2)}, u32[]{:S(2)}) async-start(bf16[8,2,16384]{2,1,0:T(2,128)(2,1)} %reshape.245), calls=%async_computation.2 | async-start | bytes 1048576 | tf_op jit(solution)/shard_map/all_to_all | solution.py:149
  20.7 0.2 reduce-window.17
  20.9 0.7 dynamic-slice_bitcast_fusion
  21.7 0.1 fusion.34
  21.8 7.9 %constant_dynamic-update-slice_fusion.2 = bf16[4096,1536]{1,0:T(8,128)(2,1)} fusion(bf16[4096,1024]{1,0:T(8,128)(2,1)} %param.11), kind=kLoop, calls=%fused_computation.78 | loop fusion | bytes 16777216
  29.7 1.6 constant_dynamic-update-slice_fusion.1
  31.3 0.8 copy-done.3
  32.1 1.7 constant_dynamic-update-slice_fusion
  33.8 1.4 all-to-all-done.1
  35.1 0.5 reshape.246
  35.7 0.7 convolution_convert_fusion
  36.4 1.0 reshape.233
  37.4 0.2 reduce-scatter.5.cloned.1.call-start
  37.7 0.5 multiply_cosine_fusion
  38.2 2.2 %fusion.3 = f32[256]{0:T(256)S(1)} fusion(bf16[256,4096]{1,0:T(8,128)(2,1)} %all-gather.3.cloned.1.call-done), kind=kLoop, calls=%fused_computation.11 | loop fusion | flops 3145472 | bytes 2098176 | tf_op jit(solution)/shard_map/reduce_sum | solution.py:78
  40.5 6.8 %fusion.6 = f32[256,1536]{1,0:T(8,128)S(1)} fusion(bf16[4096,1536]{1,0:T(8,128)(2,1)} %constant_dynamic-update-slice_fusion, bf16[256,4096]{1,0:T(8,128)(2,1)S(1)} %copy-done.4, f32[4096]{0:T(1024)S(1)} %copy-done.11, f32[256]{0:T(256)S(1)} %get-tuple-element.21), kind=kOutput, calls=%fused_computation.14 | convolution fusion | flops 3225419776 | bytes 16270336 | tf_op jit(solution)/shard_map/dot_general | solution.py:80
  47.5 0.2 copy.146
  47.7 0.9 copy-done.5
  48.6 0.5 subtract_convert_fusion.1
  49.2 0.3 slice-done
  49.5 0.1 reshape.227
  49.7 0.3 fusion.56
  50.1 2.1 %fusion.13 = (f32[2,4,256]{2,1,0:T(4,128)S(1)}, f32[2,256,256,4]{2,1,3,0:T(8,128)}) fusion(pred[256,256]{0,1:T(8,128)(4,1)S(1)} %fusion.34, bf16[256,2,4,64]{3,0,2,1:T(8,128)(2,1)S(1)} %bitcast.116, bf16[256,2,4,64]{3,0,2,1:T(8,128)(2,1)S(1)} %bitcast.118, bf16[256,2,64]{2,0,1:T(8,128)(2,1)S(1)} %get-tuple-element.11, ...), kind=kOutput, calls=%fused_computation.22 | convolution fusion | flops 137099264 | bytes 2826240 | tf_op jit(solution)/shard_map/qkgd,skd->kgqs/dot_general | solution.py:106
  52.2 8.0 %all-gather.5.cloned.1.call-done = bf16[256,4096]{1,0:T(8,128)(2,1)} async-done(((bf16[256,1024]{1,0:T(8,128)(2,1)}), bf16[256,4096]{1,0:T(8,128)(2,1)}) %all-gather.5.cloned.1.call-update) | async-done | bytes 2097168 | tf_op jit(solution)/shard_map/all_gather | solution.py:158
  60.2 6.4 %convolution_convert_fusion.6 = bf16[256,1024]{1,0:T(8,128)(2,1)S(1)} fusion(bf16[256,4096]{1,0:T(8,128)(2,1)} %all-gather.5.cloned.1.call-done, bf16[1024,4096]{1,0:T(8,128)(2,1)} %param.14), kind=kOutput, calls=%fused_computation.27 | convolution fusion | flops 2147745792 | bytes 11010048 | tf_op jit(solution)/shard_map/dot_general | solution.py:157
  66.6 0.2 copy.105
  66.8 2.4 %fusion.16 = bf16[2,128,256]{2,1,0:T(8,128)(2,1)S(1)} fusion(bf16[256,2,4,128]{0,3,2,1:T(8,128)(2,1)S(1)} %bitcast.121, f32[2,256,256,4]{2,1,3,0:T(8,128)} %get-tuple-element.23, f32[2,4,256]{2,1,0:T(4,128)S(1)} %get-tuple-element.22, pred[256,256]{0,1:T(8,128)(4,1)S(1)} %fusion.34), kind=kOutput, calls=%fused_computation.33 | convolution fusion | flops 136380416 | bytes 2826240 | tf_op jit(solution)/shard_map/kgqs,qkgd->skd/dot_general | solution.py:181
  69.3 1.6 multiply_reduce_fusion
  70.8 0.7 fusion.9
  71.6 0.5 fusion.15
  72.1 0.4 convolution_multiply_fusion
  72.6 0.2 add_convert_fusion.2
  72.8 0.1 pad_maximum_fusion.2
  72.9 0.1 copy.115
  73.0 0.8 copy.117
  73.9 0.4 copy.145
  74.3 0.4 copy.144
  74.7 0.3 add_convert_fusion
  75.0 0.3 pad_maximum_fusion.1
  75.4 0.5 copy-done.6
  75.9 13.8 %convolution_convert_fusion.4 = bf16[4096,256]{0,1:T(8,128)(2,1)} fusion(bf16[4096,1536]{1,0:T(8,128)(2,1)} %constant_dynamic-update-slice_fusion, bf16[256,256]{1,0:T(8,128)(2,1)S(1)} %copy.118, bf16[256,256]{1,0:T(8,128)(2,1)S(1)} %copy-done.6, bf16[256,1024]{1,0:T(8,128)(2,1)S(1)} %bitcast.123), kind=kOutput, calls=%fused_computation.8 | convolution fusion | flops 3224633344 | bytes 15466496 | tf_op jit(solution)/shard_map/dot_general | solution.py:198
  89.8 7.1 %fusion.2 = bf16[4096,256]{0,1:T(8,128)(2,1)} fusion(bf16[256,1024]{0,1:T(8,128)(2,1)S(1)} %bitcast.120, bf16[1024,4096]{1,0:T(8,128)(2,1)} %param.14), kind=kOutput, calls=%fused_computation.10 | convolution fusion | flops 2148532224 | bytes 11010048 | tf_op jit(solution)/shard_map/dot_general | solution.py:117
  96.9 0.8 dynamic_slice.7
  97.7 23.6 %reduce-scatter.5.cloned.1.call-done = bf16[1024,256]{0,1:T(8,128)(2,1)} async-done(((bf16[4096,256]{0,1:T(8,128)(2,1)}), bf16[1024,256]{0,1:T(8,128)(2,1)}) %reduce-scatter.5.cloned.1.call-update) | async-done | bytes 524304 | tf_op jit(solution)/shard_map/reduce_scatter | solution.py:197
  121.3 1.3 fusion.21
  122.6 5.8 %psum.7 = f32[256]{0:T(256)S(1)} all-reduce(f32[256]{0:T(256)S(1)} %fusion.21), channel_id=1, replica_groups=mesh['dp'=8,'tensor'=4] {'tensor'}, use_global_device_ids=true, to_apply=%region_11.12 | all-reduce | flops 256 | bytes 2048 | tf_op jit(solution)/shard_map/psum | solution.py:209
  128.4 26.9 %reduce-scatter.3.cloned.1.call-done = bf16[1024,256]{0,1:T(8,128)(2,1)} async-done(((bf16[4096,256]{0,1:T(8,128)(2,1)}), bf16[1024,256]{0,1:T(8,128)(2,1)}) %reduce-scatter.3.cloned.1.call-update) | async-done | bytes 524304 | tf_op jit(solution)/shard_map/reduce_scatter | solution.py:116
  155.3 2.5 %fusion.20 = (bf16[256,1024]{1,0:T(8,128)(2,1)}, bf16[256,1024]{1,0:T(8,128)(2,1)S(1)}) fusion(bf16[256,1024]{1,0:T(8,128)(2,1)S(1)} %copy-done, bf16[1024,256]{0,1:T(8,128)(2,1)} %reduce-scatter.5.cloned.1.call-done, bf16[256,1024]{1,0:T(8,128)(2,1)S(1)} %copy-done.1, f32[256]{0:T(256)S(1)} %broadcast_multiply_fusion, f32[256]{0:T(256)S(1)} %get-tuple-element.20, ...), kind=kLoop, calls=%fused_computation.37 | loop fusion | flops 3407872 | bytes 3152896 | tf_op jit(solution)/shard_map/convert_element_type | solution.py:218
  157.8 0.2 reshape.230
  158.0 0.3 fusion
  158.3 1.1 reduce.1
  159.4 0.4 reshape.243
  159.8 19.9 %all_to_all.24 = bf16[8,2,16384]{2,1,0:T(2,128)(2,1)S(1)} all-to-all(bf16[8,2,16384]{2,1,0:T(2,128)(2,1)S(1)} %reshape.243), channel_id=1, replica_groups=mesh['dp'=8,'tensor'=4] {'dp'}, dimensions={0} | all-to-all | bytes 1048576 | tf_op jit(solution)/shard_map/all_to_all | solution.py:139
  179.6 0.5 reshape.244
  180.2 0.7 convolution_convert_fusion.2
  180.8 1.0 reshape.231
  (49 shorter events, 1.0 us)
Async XLA Ops:
  7.2 31.1 %all-gather.3.cloned.1.call-start = ((), (), s32[]{:S(2)}) async-start(), calls=%async_computation.4 | async-start | bytes 2621440 | tf_op jit(solution)/shard_map/all_gather | solution.py:76
  10.2 10.5 %copy-start.12 = (s32[1,2]{1,0:T(1,128)S(1)}, s32[1,2]{1,0:T(1,128)}, u32[]{:S(2)}) copy-start(s32[1,2]{1,0:T(1,128)} %param.16) | copy-start | bytes 28
  13.4 21.7 %all-to-all-start.1 = ((bf16[8,2,16384]{2,1,0:T(2,128)(2,1)}), bf16[8,2,16384]{2,1,0:T(2,128)(2,1)S(1)}, u32[]{:S(2)}, u32[]{:S(2)}) async-start(bf16[8,2,16384]{2,1,0:T(2,128)(2,1)} %reshape.245), calls=%async_computation.2 | async-start | bytes 1048576 | tf_op jit(solution)/shard_map/all_to_all | solution.py:149
  20.6 39.6 %all-gather.5.cloned.1.call-start = ((), (), s32[]{:S(2)}) async-start(), calls=%async_computation.6 | async-start | bytes 2621440 | tf_op jit(solution)/shard_map/all_gather | solution.py:158
  21.6 14.1 %copy-start.9 = (s32[8]{0:T(128)}, s32[8]{0:T(128)S(1)}, u32[]{:S(2)}) copy-start(s32[8]{0:T(128)S(1)} %dynamic-slice_bitcast_fusion) | copy-start | bytes 100
  21.8 45.1 %copy-start.7 = (pred[256,256]{0,1:T(8,128)(4,1)}, pred[256,256]{0,1:T(8,128)(4,1)S(1)}, u32[]{:S(2)}) copy-start(pred[256,256]{0,1:T(8,128)(4,1)S(1)} %fusion.34) | copy-start | bytes 196612
  21.8 7.9 %copy-start.2 = (bf16[4096,256]{1,0:T(8,128)(2,1)S(1)}, bf16[4096,256]{1,0:T(8,128)(2,1)}, u32[]{:S(2)}) copy-start(bf16[4096,256]{1,0:T(8,128)(2,1)} %param.12) | copy-start | bytes 6291460
  29.7 2.4 %copy-start.3 = (bf16[4096,256]{1,0:T(8,128)(2,1)S(1)}, bf16[4096,256]{1,0:T(8,128)(2,1)}, u32[]{:S(2)}) copy-start(bf16[4096,256]{1,0:T(8,128)(2,1)} %param.13) | copy-start | bytes 6291460
  36.4 4.1 %copy-start.11 = (f32[4096]{0:T(1024)S(1)}, f32[4096]{0:T(1024)}, u32[]{:S(2)}) copy-start(f32[4096]{0:T(1024)} %param.10) | copy-start | bytes 49156
  37.4 83.9 %reduce-scatter.5.cloned.1.call-start = ((), (), s32[]{:S(2)}) async-start(), calls=%async_computation.7 | async-start | bytes 2621440 | tf_op jit(solution)/shard_map/reduce_scatter | solution.py:197
  38.2 2.3 %copy-start.4 = (bf16[256,4096]{1,0:T(8,128)(2,1)S(1)}, bf16[256,4096]{1,0:T(8,128)(2,1)}, u32[]{:S(2)}) copy-start(bf16[256,4096]{1,0:T(8,128)(2,1)} %all-gather.3.cloned.1.call-done) | copy-start | bytes 6291460
  47.4 1.2 copy-start.5
  48.6 0.9 slice-start
  66.8 2.4 %copy-start.13 = (f32[2,256,256,4]{2,1,3,0:T(8,128)S(1)}, f32[2,256,256,4]{2,1,3,0:T(8,128)}, u32[]{:S(2)}) copy-start(f32[2,256,256,4]{2,1,3,0:T(8,128)} %get-tuple-element.23) | copy-start | bytes 6291460
  69.2 1.6 copy-start.8
  75.0 0.9 copy-start.6
  89.7 65.6 %reduce-scatter.3.cloned.1.call-start = ((), (), s32[]{:S(2)}) async-start(), calls=%async_computation.5 | async-start | bytes 2621440 | tf_op jit(solution)/shard_map/reduce_scatter | solution.py:116
  96.9 24.4 %copy-start = (bf16[256,1024]{1,0:T(8,128)(2,1)S(1)}, bf16[256,1024]{1,0:T(8,128)(2,1)}, u32[]{:S(2)}) copy-start(bf16[256,1024]{1,0:T(8,128)(2,1)} %param.9) | copy-start | bytes 1572868
  96.9 58.4 %copy-start.1 = (bf16[256,1024]{1,0:T(8,128)(2,1)S(1)}, bf16[256,1024]{1,0:T(8,128)(2,1)}, u32[]{:S(2)}) copy-start(bf16[256,1024]{1,0:T(8,128)(2,1)} %reshape.233) | copy-start | bytes 1572868
  155.3 2.7 %copy-start.10 = (s32[8]{0:T(128)S(1)}, s32[8]{0:T(128)}, u32[]{:S(2)}) copy-start(s32[8]{0:T(128)} %copy-done.9) | copy-start | bytes 100
Sparse Core Ops, SparseCore 0:
  9.6 25.2 all-gather.2
  37.5 22.6 all-gather.4
  89.9 31.4 reduce-scatter.4
  123.9 31.3 reduce-scatter.2
where the time goes:
time: 189 us; the launch traced here: 188 us
  waiting for transfers between devices  60.6 us (32%)
  matrix products  43.8 us (23%)
  blocking collectives  25.6 us (14%)
  local copies, waits for them, and re-layouts  25.1 us (13%)
  between operations  14.2 us (8%)
  other arithmetic  11.4 us (6%)
  starting transfers between devices  7.59 us (4%)
    reduce_scatter x1, waiting for transfers between devices, per_device(): lax.psum_scatter(lax.dot_general(w_out, attended_flat, (((0,), (1,)), (()...  26.9 us
    reduce_scatter x1, waiting for transfers between devices, per_device(): lax.psum_scatter(lax.dot_general(w_joined, joined_grad, (((1,), (1,)), ((...  23.6 us
    all_to_all x1, blocking collectives, per_device(): lax.all_to_all(outgoing, 'dp', split_axis=0, concat_axis=0, tiled=True)  19.9 us
    unnamed x39, local copies, waits for them, and re-layouts  15.5 us
    dot_general x1, matrix products, per_device(): lax.dot_general(w_joined, joined_grad, (((1,), (1,)), ((), ())), preferre...  13.8 us
    all_gather x1, waiting for transfers between devices, per_device(): lax.all_gather(grad_home, 'tensor', axis=1, tiled=True)  7.99 us
    all_to_all x1, starting transfers between devices, per_device(): lax.all_to_all(returning, 'dp', split_axis=0, concat_axis=0, tiled=True)  7.25 us
    dot_general x1, matrix products, per_device(): lax.dot_general(w_out, attended_flat, (((0,), (1,)), ((), ())), preferred...  7.11 us
  transfers between devices with their start and end apart: 5, of which 4 were waited for; matrix products, arithmetic and copies ran while one was open for 23% of the time, Pallas kernels for 0%

commit v1 on v0

--- a/solution.py
+++ b/solution.py
@@ -7,6 +7,18 @@
 HEAD_SIZE = 128
 ROPE_BASE = 500000.0
 NORM_EPSILON = 1e-05
+
+
+def doubled_up(x, axis, dim):
+    ways, here, turn = (lax.axis_size(axis), lax.axis_index(axis), x.shape[dim])
+    line, have = (x, 1)
+    while have < ways:
+        line = jnp.concatenate(
+            [line, lax.ppermute(line, axis, [(d, (d - have) % ways) for d in range(ways)])],
+            axis=dim,
+        )
+        have = 2 * have
+    return jnp.roll(line, here * turn, axis=dim)
 
 
 def doc_tables(lengths_row, token_row_count):
@@ -155,7 +167,7 @@
         .reshape(token_row_count, width_part)
     )
     attended_gradient = lax.dot_general(
-        lax.all_gather(grad_home, "tensor", axis=1, tiled=True),
+        doubled_up(grad_home, "tensor", 1),
         w_out,
         (((1,), (1,)), ((), ())),
         preferred_element_type=jnp.float32,

time: 189 us -> 216 us (1.14)
  waiting for transfers between devices: 60.6 us -> 86.3 us
    ppermute x0 -> x2, waiting for transfers between devices: none -> 30.5 us  [doubled_up(): lax.ppermute(line, axis, [(d, (d - have) % ways) for d in range(ways)])]
    all_gather x1 -> x0, waiting for transfers between devices: 7.99 us -> none  [per_device(): lax.all_gather(grad_home, 'tensor', axis=1, tiled=True)]
    unnamed x39 -> x42, local copies, waits for them, and re-layouts: 15.5 us -> 15.8 us
  transfers between devices with their start and end apart: 5 -> 6, of which waited for: 4 -> 5; matrix products, arithmetic and copies ran while one was open for 23% -> 15% of each run, Pallas kernels for 0% -> 0%
where the time goes in v1:
time: 216 us
  waiting for transfers between devices  86.3 us (40%)
  matrix products  42.3 us (20%)
  local copies, waits for them, and re-layouts  25.7 us (12%)
  blocking collectives  25.6 us (12%)
  between operations  14.2 us (7%)
  other arithmetic  12 us (6%)
  starting transfers between devices  9.42 us (4%)
    ppermute x2, waiting for transfers between devices, doubled_up(): lax.ppermute(line, axis, [(d, (d - have) % ways) for d in range(ways)])  30.5 us
    reduce_scatter x1, waiting for transfers between devices, per_device(): lax.psum_scatter(lax.dot_general(w_out, attended_flat, (((0,), (1,)), (()...  27.1 us
    reduce_scatter x1, waiting for transfers between devices, per_device(): lax.psum_scatter(lax.dot_general(w_joined, joined_grad, (((1,), (1,)), ((...  24.7 us
    all_to_all x1, blocking collectives, per_device(): lax.all_to_all(outgoing, 'dp', split_axis=0, concat_axis=0, tiled=True)  19.9 us
    unnamed x42, local copies, waits for them, and re-layouts  15.8 us
    dot_general x1, matrix products, per_device(): lax.dot_general(w_joined, joined_grad, (((1,), (1,)), ((), ())), preferre...  13.8 us
    all_to_all x1, starting transfers between devices, per_device(): lax.all_to_all(returning, 'dp', split_axis=0, concat_axis=0, tiled=True)  7.25 us
    dot_general x1, matrix products, per_device(): lax.dot_general(w_out, attended_flat, (((0,), (1,)), ((), ())), preferred...  7.11 us
  transfers between devices with their start and end apart: 6, of which 5 were waited for; matrix products, arithmetic and copies ran while one was open for 15% of the time, Pallas kernels for 0%

profile of v1, /device:TPU:0, one launch (start us, length us, event | category | flops | bytes accessed | tf_op | source)
XLA Modules:
  0.0 215.6 jit_solution(16107321229920165121)
XLA Ops:
  7.2 1.3 reshape.232
  8.5 0.8 convert_reduce_fusion
  9.3 0.2 reduce-window.16
  9.5 0.4 fusion.1
  9.8 0.6 broadcast.111
  10.4 1.0 reduce
  11.4 1.2 reshape.245
  12.6 7.3 %all-to-all-start.1 = ((bf16[8,2,16384]{2,1,0:T(2,128)(2,1)}), bf16[8,2,16384]{2,1,0:T(2,128)(2,1)S(1)}, u32[]{:S(2)}, u32[]{:S(2)}) async-start(bf16[8,2,16384]{2,1,0:T(2,128)(2,1)} %reshape.245), calls=%async_computation.2 | async-start | bytes 1048576 | tf_op jit(solution)/shard_map/all_to_all | solution.py:161
  19.9 0.7 all-gather.2.cloned.1.call-update
  20.6 0.7 dynamic-slice_bitcast_fusion
  21.3 0.2 reduce-window.17
  21.5 7.9 %constant_dynamic-update-slice_fusion.2 = bf16[4096,1536]{1,0:T(8,128)(2,1)} fusion(bf16[4096,1024]{1,0:T(8,128)(2,1)} %param.11), kind=kLoop, calls=%fused_computation.81 | loop fusion | bytes 16777216
  29.4 1.7 constant_dynamic-update-slice_fusion.1
  31.1 3.2 %all-to-all-done.1 = bf16[8,2,16384]{2,1,0:T(2,128)(2,1)S(1)} async-done(((bf16[8,2,16384]{2,1,0:T(2,128)(2,1)}), bf16[8,2,16384]{2,1,0:T(2,128)(2,1)S(1)}, u32[]{:S(2)}, u32[]{:S(2)}) %all-to-all-start.1) | async-done | bytes 524320 | tf_op jit(solution)/shard_map/all_to_all | solution.py:161
  34.3 0.5 reshape.246
  34.9 1.5 convolution_convert_fusion
  36.4 1.4 reshape.233
  38.0 0.7 fusion.39
  38.7 9.5 %collective-permute-done = bf16[256,1024]{1,0:T(8,128)(2,1)S(1)} collective-permute-done((bf16[256,1024]{1,0:T(8,128)(2,1)S(1)}, bf16[256,1024]{1,0:T(8,128)(2,1)S(1)}, u32[]{:S(2)}, u32[]{:S(2)}) %collective-permute-start) | collective-permute-done | bytes 524320 | tf_op jit(solution)/shard_map/ppermute | solution.py:17
  48.3 1.8 collective-permute-start.1
  50.1 0.5 multiply_cosine_fusion
  50.6 1.6 constant_dynamic-update-slice_fusion
  52.4 21.0 %collective-permute-done.1 = bf16[256,2048]{1,0:T(8,128)(2,1)S(1)} collective-permute-done((bf16[256,2048]{1,0:T(8,128)(2,1)S(1)}, bf16[256,2048]{1,0:T(8,128)(2,1)S(1)}, u32[]{:S(2)}, u32[]{:S(2)}) %collective-permute-start.1) | collective-permute-done | bytes 1048608 | tf_op jit(solution)/shard_map/ppermute | solution.py:17
  73.6 5.7 %fusion.16 = bf16[256,1024]{1,0:T(8,128)(2,1)S(1)} fusion(bf16[1024,4096]{1,0:T(8,128)(2,1)} %param.14, bf16[256,8192]{1,0:T(8,128)(2,1)S(1)} %constant_dynamic-update-slice_fusion.3, s32[]{:T(128)S(6)} %select_n.32), kind=kOutput, calls=%fused_computation.29 | convolution fusion | flops 2147745792 | bytes 11010052 | tf_op jit(solution)/shard_map/dot_general | solution.py:169
  79.4 0.2 copy.105
  79.6 2.2 %fusion.3 = f32[256]{0:T(256)S(1)} fusion(bf16[256,4096]{1,0:T(8,128)(2,1)} %all-gather.2.cloned.1.call-done), kind=kLoop, calls=%fused_computation.11 | loop fusion | flops 3145472 | bytes 2098176 | tf_op jit(solution)/shard_map/reduce_sum | solution.py:90
  81.9 6.7 %fusion.6 = f32[256,1536]{1,0:T(8,128)S(1)} fusion(bf16[4096,1536]{1,0:T(8,128)(2,1)} %constant_dynamic-update-slice_fusion, bf16[256,4096]{1,0:T(8,128)(2,1)S(1)} %copy-done.3, f32[4096]{0:T(1024)S(1)} %copy-done.11, f32[256]{0:T(256)S(1)} %get-tuple-element.21), kind=kOutput, calls=%fused_computation.14 | convolution fusion | flops 3225419776 | bytes 16270336 | tf_op jit(solution)/shard_map/dot_general | solution.py:92
  88.8 0.2 copy.146
  89.0 0.9 copy-done.4
  89.8 0.5 subtract_convert_fusion.1
  90.5 0.3 slice-done
  90.8 0.1 reshape.227
  90.9 0.3 fusion.62
  91.4 1.7 fusion.15
  93.1 1.3 fusion.21
  94.4 1.5 multiply_reduce_fusion
  95.9 0.7 fusion.9
  96.6 0.5 fusion.20
  97.2 0.4 convolution_multiply_fusion
  97.7 0.2 add_convert_fusion.2
  98.1 0.8 copy.117
  99.0 0.4 copy.145
  99.4 0.4 copy.144
  99.8 0.3 add_convert_fusion
  100.1 0.3 pad_maximum_fusion.2
  100.5 0.5 copy-done.6
  101.0 13.8 %convolution_convert_fusion.4 = bf16[4096,256]{0,1:T(8,128)(2,1)} fusion(bf16[4096,1536]{1,0:T(8,128)(2,1)} %constant_dynamic-update-slice_fusion, bf16[256,256]{1,0:T(8,128)(2,1)S(1)} %copy.118, bf16[256,256]{1,0:T(8,128)(2,1)S(1)} %copy-done.6, bf16[256,1024]{1,0:T(8,128)(2,1)S(1)} %bitcast.122), kind=kOutput, calls=%fused_computation.8 | convolution fusion | flops 3224633344 | bytes 15466496 | tf_op jit(solution)/shard_map/dot_general | solution.py:210
  114.8 0.3 reduce-scatter.3.cloned.1.call-start
  115.1 0.7 copy-done.5
  115.8 7.1 %fusion.2 = bf16[4096,256]{0,1:T(8,128)(2,1)} fusion(bf16[256,1024]{0,1:T(8,128)(2,1)S(1)} %bitcast.119, bf16[1024,4096]{1,0:T(8,128)(2,1)} %param.14), kind=kOutput, calls=%fused_computation.10 | convolution fusion | flops 2148532224 | bytes 11010048 | tf_op jit(solution)/shard_map/dot_general | solution.py:129
  123.0 0.7 dynamic_slice.11
  123.7 24.7 %reduce-scatter.5.cloned.1.call-done = bf16[1024,256]{0,1:T(8,128)(2,1)} async-done(((bf16[4096,256]{0,1:T(8,128)(2,1)}), bf16[1024,256]{0,1:T(8,128)(2,1)}) %reduce-scatter.5.cloned.1.call-update) | async-done | bytes 524304 | tf_op jit(solution)/shard_map/reduce_scatter | solution.py:209
  148.5 1.3 fusion.26
  149.7 5.8 %psum.7 = f32[256]{0:T(256)S(1)} all-reduce(f32[256]{0:T(256)S(1)} %fusion.26), channel_id=1, replica_groups=mesh['dp'=8,'tensor'=4] {'tensor'}, use_global_device_ids=true, to_apply=%region_11.12 | all-reduce | flops 256 | bytes 2048 | tf_op jit(solution)/shard_map/psum | solution.py:221
  155.5 27.1 %reduce-scatter.3.cloned.1.call-done = bf16[1024,256]{0,1:T(8,128)(2,1)} async-done(((bf16[4096,256]{0,1:T(8,128)(2,1)}), bf16[1024,256]{0,1:T(8,128)(2,1)}) %reduce-scatter.3.cloned.1.call-update) | async-done | bytes 524304 | tf_op jit(solution)/shard_map/reduce_scatter | solution.py:128
  182.6 2.5 %fusion.25 = (bf16[256,1024]{1,0:T(8,128)(2,1)}, bf16[256,1024]{1,0:T(8,128)(2,1)S(1)}) fusion(bf16[256,1024]{1,0:T(8,128)(2,1)S(1)} %copy-done, bf16[1024,256]{0,1:T(8,128)(2,1)} %reduce-scatter.5.cloned.1.call-done, bf16[256,1024]{1,0:T(8,128)(2,1)S(1)} %reshape.233, f32[256]{0:T(256)S(1)} %broadcast_multiply_fusion, f32[256]{0:T(256)S(1)} %get-tuple-element.20, ...), kind=kLoop, calls=%fused_computation.39 | loop fusion | flops 3407872 | bytes 3152896 | tf_op jit(solution)/shard_map/convert_element_type | solution.py:230
  185.1 0.2 reshape.230
  185.3 0.3 fusion
  185.6 1.0 reduce.1
  186.6 0.4 reshape.243
  187.0 19.9 %all_to_all.24 = bf16[8,2,16384]{2,1,0:T(2,128)(2,1)S(1)} all-to-all(bf16[8,2,16384]{2,1,0:T(2,128)(2,1)S(1)} %reshape.243), channel_id=1, replica_groups=mesh['dp'=8,'tensor'=4] {'dp'}, dimensions={0} | all-to-all | bytes 1048576 | tf_op jit(solution)/shard_map/all_to_all | solution.py:151
  206.9 0.5 reshape.244
  207.4 0.7 convolution_convert_fusion.2
  208.1 1.0 reshape.231
  (55 shorter events, 1.6 us)
Async XLA Ops:
  9.8 11.5 %copy-start.12 = (s32[1,2]{1,0:T(1,128)S(1)}, s32[1,2]{1,0:T(1,128)}, u32[]{:S(2)}) copy-start(s32[1,2]{1,0:T(1,128)} %param.16) | copy-start | bytes 28
  12.6 21.7 %all-to-all-start.1 = ((bf16[8,2,16384]{2,1,0:T(2,128)(2,1)}), bf16[8,2,16384]{2,1,0:T(2,128)(2,1)S(1)}, u32[]{:S(2)}, u32[]{:S(2)}) async-start(bf16[8,2,16384]{2,1,0:T(2,128)(2,1)} %reshape.245), calls=%async_computation.2 | async-start | bytes 1048576 | tf_op jit(solution)/shard_map/all_to_all | solution.py:161
  19.9 59.8 %all-gather.2.cloned.1.call-start = ((), (), s32[]{:S(2)}) async-start(), calls=%async_computation.4 | async-start | bytes 2621440 | tf_op jit(solution)/shard_map/all_gather | solution.py:88
  20.6 127.9 %reduce-scatter.5.cloned.1.call-start = ((), (), s32[]{:S(2)}) async-start(), calls=%async_computation.6 | async-start | bytes 2621440 | tf_op jit(solution)/shard_map/reduce_scatter | solution.py:209
  21.3 13.5 %copy-start.9 = (s32[8]{0:T(128)}, s32[8]{0:T(128)S(1)}, u32[]{:S(2)}) copy-start(s32[8]{0:T(128)S(1)} %dynamic-slice_bitcast_fusion) | copy-start | bytes 100
  21.5 7.9 %copy-start.1 = (bf16[4096,256]{1,0:T(8,128)(2,1)S(1)}, bf16[4096,256]{1,0:T(8,128)(2,1)}, u32[]{:S(2)}) copy-start(bf16[4096,256]{1,0:T(8,128)(2,1)} %param.12) | copy-start | bytes 6291460
  36.4 14.3 %copy-start.2 = (bf16[4096,256]{1,0:T(8,128)(2,1)S(1)}, bf16[4096,256]{1,0:T(8,128)(2,1)}, u32[]{:S(2)}) copy-start(bf16[4096,256]{1,0:T(8,128)(2,1)} %param.13) | copy-start | bytes 6291460
  37.8 10.4 %collective-permute-start = (bf16[256,1024]{1,0:T(8,128)(2,1)S(1)}, bf16[256,1024]{1,0:T(8,128)(2,1)S(1)}, u32[]{:S(2)}, u32[]{:S(2)}) collective-permute-start(bf16[256,1024]{1,0:T(8,128)(2,1)S(1)} %reshape.233), channel_id=1, source_target_pairs={{0,3},{1,0},{2,1},{3,2},{4,7},{5,4},{6,5},{7,6},{8,11},{9,8},{10,9... | collective-permute-start | bytes 1572872 | tf_op jit(solution)/shard_map/ppermute | solution.py:17
  48.3 25.1 %collective-permute-start.1 = (bf16[256,2048]{1,0:T(8,128)(2,1)S(1)}, bf16[256,2048]{1,0:T(8,128)(2,1)S(1)}, u32[]{:S(2)}, u32[]{:S(2)}) collective-permute-start(bf16[256,2048]{1,0:T(8,128)(2,1)S(1)} %pad_maximum_fusion), channel_id=1, source_target_pairs={{0,2},{1,3},{2,0},{3,1},{4,6},{5,7},{6,4},{7,5},{8,10},{9,11},{10,... | collective-permute-start | bytes 3145736 | tf_op jit(solution)/shard_map/ppermute | solution.py:17
  79.4 2.5 %copy-start.11 = (f32[4096]{0:T(1024)S(1)}, f32[4096]{0:T(1024)}, u32[]{:S(2)}) copy-start(f32[4096]{0:T(1024)} %param.10) | copy-start | bytes 49156
  79.6 2.3 %copy-start.3 = (bf16[256,4096]{1,0:T(8,128)(2,1)S(1)}, bf16[256,4096]{1,0:T(8,128)(2,1)}, u32[]{:S(2)}) copy-start(bf16[256,4096]{1,0:T(8,128)(2,1)} %all-gather.2.cloned.1.call-done) | copy-start | bytes 6291460
  88.6 1.2 copy-start.4
  89.8 0.9 slice-start
  91.3 1.8 copy-start.8
  96.6 1.0 copy-start.7
  100.1 0.9 copy-start.6
  114.8 1.0 copy-start.5
  114.8 67.8 %reduce-scatter.3.cloned.1.call-start = ((), (), s32[]{:S(2)}) async-start(), calls=%async_computation.5 | async-start | bytes 2621440 | tf_op jit(solution)/shard_map/reduce_scatter | solution.py:128
  123.0 25.5 %copy-start = (bf16[256,1024]{1,0:T(8,128)(2,1)S(1)}, bf16[256,1024]{1,0:T(8,128)(2,1)}, u32[]{:S(2)}) copy-start(bf16[256,1024]{1,0:T(8,128)(2,1)} %param.9) | copy-start | bytes 1572868
  182.6 2.7 %copy-start.10 = (s32[8]{0:T(128)S(1)}, s32[8]{0:T(128)}, u32[]{:S(2)}) copy-start(s32[8]{0:T(128)} %copy-done.9) | copy-start | bytes 100
Sparse Core Ops, SparseCore 0:
  22.2 26.0 all-gather.1
  115.0 33.4 reduce-scatter.4
  151.1 31.4 reduce-scatter.2
